TPU v7x, 256 devices: a whole 4x4x8 slice. The times are simulated.
256 devices in a mesh: prow: 64 (over x, z, core), pcol: 4 (over y).
Axes of the slice: x: 4, y: 4, z: 8, core: 2. Of those that a mesh axis runs over, the one named last changes fastest.
Arguments:
- right_side: float32 [512, 65536], P('pcol', 'prow'), may hold values from -6 to 6
- factor: float32 [65536, 2048], P('prow', 'pcol'), may hold values from -0.125 to 0.125
- inverses: float32 [2048, 512], replicated, as said below
Outputs:
- solved: float32 [512, 65536], P('pcol', 'prow')
Inputs may be any that keep to these rules, and one draw needn't show every extreme that they name: Each 512 x 512 block of inverses is lower triangular with a positive diagonal.
All inputs are finite; a program needn't handle non-finite values.
Results may differ from a plain program's by a relative error of at most 0.0001.
Values sent between devices are 32-bit elements; how exact they have to be, the bound alone decides.
No kernel may reach another device: no remote copies, remote signals or barrier semaphores. Data moves between devices by JAX's collectives and lax.ppermute only.
A program may use at most 64 MiB of HBM per device.

v0:
```python
import jax
import jax.numpy as jnp
from jax import lax
from jax.sharding import PartitionSpec as P


def spread(block, axis, source):
    block = jnp.where(lax.axis_index(axis) == source, block, jnp.zeros_like(block))
    return lax.psum(block, axis)


def contract(left, right):
    return lax.dot_general(
        left,
        right,
        (((1,), (1,)), ((), ())),
        precision=lax.Precision.HIGHEST,
        preferred_element_type=jnp.float32,
    )


def per_device(right_side, factor, inverses):
    block = factor.shape[1]
    rhs_width = right_side.shape[0]
    sections = lax.axis_size("pcol")
    all_samples = rhs_width * sections
    row_at = lax.axis_index("prow")
    col_at = lax.axis_index("pcol")
    top_block = factor[:block]
    panel_own = jnp.zeros((all_samples, block), jnp.float32)
    solved_head = jnp.zeros((rhs_width, block), jnp.float32)
    own_panels = []
    for section in range(sections):
        current = right_side[:, :block]
        if section > 0:
            current = current - lax.psum_scatter(
                contract(panel_own, top_block), "pcol", scatter_dimension=0, tiled=True
            )
        block_inverse = inverses[section * block : (section + 1) * block]
        solved_part = contract(current, block_inverse)
        solved_head = jnp.where(row_at == section, solved_part, solved_head)
        gathered = lax.all_gather(solved_part, "pcol", axis=0, tiled=True)
        panel_full = spread(gathered, "prow", section)
        panel_own = jnp.where(col_at == section, panel_full, panel_own)
        own_panels.append(lax.dynamic_slice_in_dim(panel_full, col_at * rhs_width, rhs_width, 0))
    updated = right_side - lax.psum_scatter(
        contract(panel_own, factor), "pcol", scatter_dimension=0, tiled=True
    )
    head_block = jnp.where(row_at < sections, solved_head, updated[:, :block])
    return jnp.concatenate([head_block, updated[:, block:]], axis=1)


def solution(mesh):
    return jax.shard_map(
        per_device,
        mesh=mesh,
        in_specs=(P("pcol", "prow"), P("prow", "pcol"), P()),
        out_specs=P("pcol", "prow"),
        check_vma=False,
    )
```

profile of v0, /device:TPU:1, one launch (start us, length us, event | category | flops | bytes accessed | tf_op | source)
XLA Modules:
  0.0 1011.9 jit_solution(13477425533814743867)
XLA Ops:
  6.5 0.0 all-gather.5.cloned.1.call-start
  6.5 3.2 fusion.8
  9.7 0.0 copy-start
  9.7 0.0 all-gather.5.cloned.1.call-update
  9.7 0.0 all-reduce.5.cloned.1.call-start
  9.8 29.5 %all-gather.5.cloned.1.call-done = f32[512,512]{1,0:T(8,128)} async-done(((f32[128,512]{1,0:T(8,128)}), f32[512,512]{1,0:T(8,128)}) %all-gather.5.cloned.1.call-update) | async-done | bytes 1048592 | tf_op jit(solution)/shard_map/all_gather | solution.py:42
  39.3 1.1 broadcast_select_fusion.3
  40.4 0.0 all-reduce.5.cloned.1.call-update
  40.4 0.0 reduce-scatter.5.cloned.1.call-start
  40.5 0.0 copy-start.1
  40.5 187.1 %all-reduce.5.cloned.1.call-done = f32[512,512]{1,0:T(8,128)} async-done(((f32[512,512]{1,0:T(8,128)}), f32[512,512]{1,0:T(8,128)}) %all-reduce.5.cloned.1.call-update) | async-done | bytes 1048592 | tf_op jit(solution)/shard_map/psum | solution.py:9
  227.6 0.0 copy-done
  227.6 4.1 fusion.10
  231.7 0.0 reduce-scatter.5.cloned.1.call-update
  231.7 0.0 all-gather.7.cloned.1.call-start
  231.8 22.7 %reduce-scatter.5.cloned.1.call-done = f32[128,512]{1,0:T(8,128)} async-done(((f32[512,512]{1,0:T(8,128)}), f32[128,512]{1,0:T(8,128)}) %reduce-scatter.5.cloned.1.call-update) | async-done | bytes 262160 | tf_op jit(solution)/shard_map/reduce_scatter | solution.py:36
  254.5 0.0 copy-done.1
  254.5 3.2 fusion.6
  257.7 0.0 all-gather.7.cloned.1.call-update
  257.7 0.0 all-reduce.7.cloned.1.call-start
  257.8 26.9 %all-gather.7.cloned.1.call-done = f32[512,512]{1,0:T(8,128)} async-done(((f32[128,512]{1,0:T(8,128)}), f32[512,512]{1,0:T(8,128)}) %all-gather.7.cloned.1.call-update) | async-done | bytes 1048592 | tf_op jit(solution)/shard_map/all_gather | solution.py:42
  284.6 2.3 broadcast_select_fusion.2
  286.9 0.0 all-reduce.7.cloned.1.call-update
  286.9 0.0 reduce-scatter.7.cloned.1.call-start
  287.0 185.8 %all-reduce.7.cloned.1.call-done = f32[512,512]{1,0:T(8,128)} async-done(((f32[512,512]{1,0:T(8,128)}), f32[512,512]{1,0:T(8,128)}) %all-reduce.7.cloned.1.call-update) | async-done | bytes 1048592 | tf_op jit(solution)/shard_map/psum | solution.py:9
  472.8 1.4 select_select_fusion
  474.2 2.8 fusion.14
  477.1 0.0 reduce-scatter.7.cloned.1.call-update
  477.1 0.0 all-gather.9.cloned.1.call-start
  477.1 22.7 %reduce-scatter.7.cloned.1.call-done = f32[128,512]{1,0:T(8,128)} async-done(((f32[512,512]{1,0:T(8,128)}), f32[128,512]{1,0:T(8,128)}) %reduce-scatter.7.cloned.1.call-update) | async-done | bytes 262160 | tf_op jit(solution)/shard_map/reduce_scatter | solution.py:36
  499.9 3.3 fusion.4
  503.1 0.0 all-gather.9.cloned.1.call-update
  503.2 0.0 all-reduce.9.cloned.1.call-start
  503.2 26.9 %all-gather.9.cloned.1.call-done = f32[512,512]{1,0:T(8,128)} async-done(((f32[128,512]{1,0:T(8,128)}), f32[512,512]{1,0:T(8,128)}) %all-gather.9.cloned.1.call-update) | async-done | bytes 1048592 | tf_op jit(solution)/shard_map/all_gather | solution.py:42
  530.2 1.1 broadcast_select_fusion.1
  531.2 0.0 all-reduce.9.cloned.1.call-update
  531.3 0.0 reduce-scatter.9.cloned.1.call-start
  531.3 187.1 %all-reduce.9.cloned.1.call-done = f32[512,512]{1,0:T(8,128)} async-done(((f32[512,512]{1,0:T(8,128)}), f32[512,512]{1,0:T(8,128)}) %all-reduce.9.cloned.1.call-update) | async-done | bytes 1048592 | tf_op jit(solution)/shard_map/psum | solution.py:9
  718.4 2.8 fusion.12
  721.3 0.0 reduce-scatter.9.cloned.1.call-update
  721.3 0.0 all-gather.11.cloned.1.call-start
  721.4 25.3 %reduce-scatter.9.cloned.1.call-done = f32[128,512]{1,0:T(8,128)} async-done(((f32[512,512]{1,0:T(8,128)}), f32[128,512]{1,0:T(8,128)}) %reduce-scatter.9.cloned.1.call-update) | async-done | bytes 262160 | tf_op jit(solution)/shard_map/reduce_scatter | solution.py:36
  746.6 3.3 fusion.2
  749.9 0.0 all-gather.11.cloned.1.call-update
  749.9 0.0 all-reduce.11.cloned.1.call-start
  750.0 26.9 %all-gather.11.cloned.1.call-done = f32[512,512]{1,0:T(8,128)} async-done(((f32[128,512]{1,0:T(8,128)}), f32[512,512]{1,0:T(8,128)}) %all-gather.11.cloned.1.call-update) | async-done | bytes 1048592 | tf_op jit(solution)/shard_map/all_gather | solution.py:42
  776.8 1.1 broadcast_select_fusion
  777.9 0.0 all-reduce.11.cloned.1.call-update
  777.9 0.2 reduce-scatter.11.cloned.1.call-start
  778.2 186.9 %all-reduce.11.cloned.1.call-done = f32[512,512]{1,0:T(8,128)} async-done(((f32[512,512]{1,0:T(8,128)}), f32[512,512]{1,0:T(8,128)}) %all-reduce.11.cloned.1.call-update) | async-done | bytes 1048592 | tf_op jit(solution)/shard_map/psum | solution.py:9
  965.1 4.9 fusion
  970.0 0.0 copy-start.2
  970.0 0.0 copy-start.6
  970.0 0.0 reduce-scatter.11.cloned.1.call-update
  970.1 32.8 %reduce-scatter.11.cloned.1.call-done = f32[128,1024]{1,0:T(8,128)} async-done(((f32[512,1024]{1,0:T(8,128)}), f32[128,1024]{1,0:T(8,128)}) %reduce-scatter.11.cloned.1.call-update) | async-done | bytes 524304 | tf_op jit(solution)/shard_map/reduce_scatter | solution.py:46
  1002.9 0.0 copy-done.2
  1002.9 1.1 sub.15
  1004.0 0.0 copy-done.3
  1004.0 0.0 copy-done.4
  1004.0 0.0 copy-done.5
  1004.1 0.0 copy-done.6
  1004.1 0.2 slice_select_fusion
  1004.2 0.0 copy-start.7
  1004.2 0.8 copy-done.7
  (4 shorter events, 0.0 us)
Async XLA Ops:
  6.5 32.8 %all-gather.5.cloned.1.call-start = ((), (), s32[]{:S(2)}) async-start(), calls=%async_computation.4 | async-start | bytes 1310720 | tf_op jit(solution)/shard_map/all_gather | solution.py:42
  9.7 217.9 %copy-start = (f32[1024,512]{1,0:T(8,128)S(1)}, f32[1024,512]{1,0:T(8,128)}, u32[]{:S(2)}) copy-start(f32[1024,512]{1,0:T(8,128)} %param.4) | copy-start | bytes 6291460
  9.7 217.9 %all-reduce.5.cloned.1.call-start = ((), (), s32[]{:S(2)}) async-start(), calls=%async_computation.5 | async-start | bytes 2097152 | tf_op jit(solution)/shard_map/psum | solution.py:9
  40.4 214.1 %reduce-scatter.5.cloned.1.call-start = ((), (), s32[]{:S(2)}) async-start(), calls=%async_computation.6 | async-start | bytes 1310720 | tf_op jit(solution)/shard_map/reduce_scatter | solution.py:36
  40.5 214.0 %copy-start.1 = (f32[128,1024]{1,0:T(8,128)S(1)}, f32[128,1024]{1,0:T(8,128)}, u32[]{:S(2)}) copy-start(f32[128,1024]{1,0:T(8,128)} %param.3) | copy-start | bytes 1572868
  231.7 52.9 %all-gather.7.cloned.1.call-start = ((), (), s32[]{:S(2)}) async-start(), calls=%async_computation.7 | async-start | bytes 1310720 | tf_op jit(solution)/shard_map/all_gather | solution.py:42
  257.7 215.0 %all-reduce.7.cloned.1.call-start = ((), (), s32[]{:S(2)}) async-start(), calls=%async_computation.8 | async-start | bytes 2097152 | tf_op jit(solution)/shard_map/psum | solution.py:9
  286.9 212.9 %reduce-scatter.7.cloned.1.call-start = ((), (), s32[]{:S(2)}) async-start(), calls=%async_computation.9 | async-start | bytes 1310720 | tf_op jit(solution)/shard_map/reduce_scatter | solution.py:36
  477.1 53.1 %all-gather.9.cloned.1.call-start = ((), (), s32[]{:S(2)}) async-start(), calls=%async_computation.10 | async-start | bytes 1310720 | tf_op jit(solution)/shard_map/all_gather | solution.py:42
  503.2 215.3 %all-reduce.9.cloned.1.call-start = ((), (), s32[]{:S(2)}) async-start(), calls=%async_computation.11 | async-start | bytes 2097152 | tf_op jit(solution)/shard_map/psum | solution.py:9
  531.3 215.3 %reduce-scatter.9.cloned.1.call-start = ((), (), s32[]{:S(2)}) async-start(), calls=%async_computation.12 | async-start | bytes 1310720 | tf_op jit(solution)/shard_map/reduce_scatter | solution.py:36
  721.3 55.5 %all-gather.11.cloned.1.call-start = ((), (), s32[]{:S(2)}) async-start(), calls=%async_computation.13 | async-start | bytes 1310720 | tf_op jit(solution)/shard_map/all_gather | solution.py:42
  749.9 215.2 %all-reduce.11.cloned.1.call-start = ((), (), s32[]{:S(2)}) async-start(), calls=%async_computation.14 | async-start | bytes 2097152 | tf_op jit(solution)/shard_map/psum | solution.py:9
  777.9 225.0 %reduce-scatter.11.cloned.1.call-start = ((), (), s32[]{:S(2)}) async-start(), calls=%async_computation.15 | async-start | bytes 2621440 | tf_op jit(solution)/shard_map/reduce_scatter | solution.py:46
  970.0 32.9 %copy-start.2 = (f32[128,1024]{1,0:T(8,128)S(1)}, f32[128,1024]{1,0:T(8,128)}, u32[]{:S(2)}) copy-start(f32[128,1024]{1,0:T(8,128)} %param.3) | copy-start | bytes 1572868
  970.0 34.0 %copy-start.3 = (f32[128,512]{1,0:T(8,128)S(1)}, f32[128,512]{1,0:T(8,128)}, u32[]{:S(2)}) copy-start(f32[128,512]{1,0:T(8,128)} %fusion.6) | copy-start | bytes 786436
  970.0 34.0 %copy-start.4 = (f32[128,512]{1,0:T(8,128)S(1)}, f32[128,512]{1,0:T(8,128)}, u32[]{:S(2)}) copy-start(f32[128,512]{1,0:T(8,128)} %fusion.4) | copy-start | bytes 786436
  970.0 34.0 %copy-start.5 = (f32[128,512]{1,0:T(8,128)S(1)}, f32[128,512]{1,0:T(8,128)}, u32[]{:S(2)}) copy-start(f32[128,512]{1,0:T(8,128)} %fusion.2) | copy-start | bytes 786436
  970.0 34.0 %copy-start.6 = (f32[128,512]{1,0:T(8,128)S(1)}, f32[128,512]{1,0:T(8,128)}, u32[]{:S(2)}) copy-start(f32[128,512]{1,0:T(8,128)} %fusion.8) | copy-start | bytes 786436
  1004.2 0.8 copy-start.7
Sparse Core Ops, SparseCore 0:
  9.9 29.4 all-gather.4
  42.8 184.8 all-reduce.4
  231.8 22.6 reduce-scatter.4
  257.8 26.7 all-gather.6
  287.9 184.8 all-reduce.6
  477.2 22.6 reduce-scatter.6
  503.3 26.8 all-gather.8
  533.6 184.8 all-reduce.8
  721.4 25.1 reduce-scatter.8
  750.0 26.7 all-gather.10
  780.3 184.8 all-reduce.10
  970.2 32.6 reduce-scatter.10
where the time goes:
time: 1010 us
  waiting for transfers between devices  961 us (95%)
  matrix products  27.6 us (3%)
  between operations  13.7 us (1%)
    psum x4, waiting for transfers between devices, spread(): return lax.psum(block, axis)  747 us
    all_gather x4, waiting for transfers between devices, per_device(): gathered = lax.all_gather(solved_part, 'pcol', axis=0, tiled=True)  110 us
    reduce_scatter x3, waiting for transfers between devices, per_device(): lax.psum_scatter(contract(panel_own, top_block), 'pcol', scatter_dimensio...  70.7 us
    reduce_scatter x1, waiting for transfers between devices, per_device(): lax.psum_scatter(contract(panel_own, factor), 'pcol', scatter_dimension=0...  32.8 us
    dot_general x8, matrix products, contract(): lax.dot_general(left, right, (((1,), (1,)), ((), ())), precision=lax.Prec...  27.6 us
  transfers between devices with their start and end apart: 12, of which 12 were waited for; matrix products, arithmetic and copies ran while one was open for 0% of the time, Pallas kernels for 0%

commit v1 on v0

--- a/solution.py
+++ b/solution.py
@@ -39,7 +39,9 @@
         block_inverse = inverses[section * block : (section + 1) * block]
         solved_part = contract(current, block_inverse)
         solved_head = jnp.where(row_at == section, solved_part, solved_head)
-        gathered = lax.all_gather(solved_part, "pcol", axis=0, tiled=True)
+        gathered = jnp.concatenate(
+            lax.all_to_all(jnp.stack([solved_part] * lax.axis_size("pcol")), "pcol", 0, 0), axis=0
+        )
         panel_full = spread(gathered, "prow", section)
         panel_own = jnp.where(col_at == section, panel_full, panel_own)
         own_panels.append(lax.dynamic_slice_in_dim(panel_full, col_at * rhs_width, rhs_width, 0))

time: 1010 us -> 970 us (0.960)
  waiting for transfers between devices: 961 us -> 900 us
  starting transfers between devices: 0.64 us -> 17.5 us
    all_gather x4 -> x0, waiting for transfers between devices: 110 us -> none  [per_device(): gathered = lax.all_gather(solved_part, 'pcol', axis=0, tiled=True)]
    all_to_all x0 -> x4, waiting for transfers between devices: none -> 52.6 us  [per_device(): lax.all_to_all(jnp.stack([solved_part] * lax.axis_size('pcol')), 'pcol',...]
    all_to_all x0 -> x4, starting transfers between devices: none -> 17 us  [per_device(): lax.all_to_all(jnp.stack([solved_part] * lax.axis_size('pcol')), 'pcol',...]
where the time goes in v1:
time: 970 us; the launch traced here: 969 us
  waiting for transfers between devices  900 us (93%)
  matrix products  24.7 us (3%)
  starting transfers between devices  17.5 us (2%)
  between operations  13.7 us (1%)
    psum x4, waiting for transfers between devices, spread(): return lax.psum(block, axis)  743 us
    reduce_scatter x3, waiting for transfers between devices, per_device(): lax.psum_scatter(contract(panel_own, top_block), 'pcol', scatter_dimensio...  70.8 us
    all_to_all x4, waiting for transfers between devices, per_device(): lax.all_to_all(jnp.stack([solved_part] * lax.axis_size('pcol')), 'pcol',...  52.6 us
    reduce_scatter x1, waiting for transfers between devices, per_device(): lax.psum_scatter(contract(panel_own, factor), 'pcol', scatter_dimension=0...  32.8 us
    dot_general x8, matrix products, contract(): lax.dot_general(left, right, (((1,), (1,)), ((), ())), precision=lax.Prec...  24.7 us
  transfers between devices with their start and end apart: 12, of which 12 were waited for; matrix products, arithmetic and copies ran while one was open for 0% of the time, Pallas kernels for 0%

profile of v1, /device:TPU:1, one launch (start us, length us, event | category | flops | bytes accessed | tf_op | source)
XLA Modules:
  0.0 969.2 jit_solution(14496978178855155308)
XLA Ops:
  6.5 2.5 fusion.8
  9.0 0.0 copy-start.7
  9.0 1.1 stack.8
  10.1 0.0 copy-done.7
  10.1 5.0 all-to-all-start
  15.1 0.0 all-reduce.5.cloned.1.call-start
  15.2 13.4 %all-to-all-done = f32[4,128,512]{2,1,0:T(8,128)S(1)} async-done(((f32[4,128,512]{2,1,0:T(8,128)}), f32[4,128,512]{2,1,0:T(8,128)S(1)}, u32[]{:S(2)}, u32[]{:S(2)}) %all-to-all-start) | async-done | bytes 1048608 | tf_op jit(solution)/shard_map/all_to_all | solution.py:43
  28.6 1.1 broadcast_select_fusion.3
  29.7 0.0 all-reduce.5.cloned.1.call-update
  29.7 0.0 reduce-scatter.5.cloned.1.call-start
  29.8 0.0 copy-start.1
  29.8 186.6 %all-reduce.5.cloned.1.call-done = f32[512,512]{1,0:T(8,128)} async-done(((f32[512,512]{1,0:T(8,128)}), f32[512,512]{1,0:T(8,128)}) %all-reduce.5.cloned.1.call-update) | async-done | bytes 1048592 | tf_op jit(solution)/shard_map/psum | solution.py:9
  216.3 0.0 copy-done
  216.3 4.1 fusion.10
  220.4 0.0 reduce-scatter.5.cloned.1.call-update
  220.4 22.8 %reduce-scatter.5.cloned.1.call-done = f32[128,512]{1,0:T(8,128)} async-done(((f32[512,512]{1,0:T(8,128)}), f32[128,512]{1,0:T(8,128)}) %reduce-scatter.5.cloned.1.call-update) | async-done | bytes 262160 | tf_op jit(solution)/shard_map/reduce_scatter | solution.py:36
  243.2 0.0 copy-done.1
  243.2 2.5 fusion.6
  245.7 1.1 stack.9
  246.8 3.5 all-to-all-start.1
  250.3 0.0 all-reduce.7.cloned.1.call-start
  250.4 13.0 %all-to-all-done.1 = f32[4,128,512]{2,1,0:T(8,128)S(1)} async-done(((f32[4,128,512]{2,1,0:T(8,128)}), f32[4,128,512]{2,1,0:T(8,128)S(1)}, u32[]{:S(2)}, u32[]{:S(2)}) %all-to-all-start.1) | async-done | bytes 1048608 | tf_op jit(solution)/shard_map/all_to_all | solution.py:43
  263.4 1.1 broadcast_select_fusion.2
  264.5 0.0 all-reduce.7.cloned.1.call-update
  264.5 0.0 reduce-scatter.7.cloned.1.call-start
  264.6 185.5 %all-reduce.7.cloned.1.call-done = f32[512,512]{1,0:T(8,128)} async-done(((f32[512,512]{1,0:T(8,128)}), f32[512,512]{1,0:T(8,128)}) %all-reduce.7.cloned.1.call-update) | async-done | bytes 1048592 | tf_op jit(solution)/shard_map/psum | solution.py:9
  450.0 1.4 select_select_fusion
  451.5 2.8 fusion.14
  454.3 0.0 reduce-scatter.7.cloned.1.call-update
  454.3 22.8 %reduce-scatter.7.cloned.1.call-done = f32[128,512]{1,0:T(8,128)} async-done(((f32[512,512]{1,0:T(8,128)}), f32[128,512]{1,0:T(8,128)}) %reduce-scatter.7.cloned.1.call-update) | async-done | bytes 262160 | tf_op jit(solution)/shard_map/reduce_scatter | solution.py:36
  477.1 2.6 fusion.4
  479.7 0.0 copy-start.3
  479.7 0.7 copy-done.3
  480.4 1.1 stack.10
  481.5 4.2 all-to-all-start.2
  485.8 0.0 all-reduce.9.cloned.1.call-start
  485.8 13.1 %all-to-all-done.2 = f32[4,128,512]{2,1,0:T(8,128)} async-done(((f32[4,128,512]{2,1,0:T(8,128)}), f32[4,128,512]{2,1,0:T(8,128)}, u32[]{:S(2)}, u32[]{:S(2)}) %all-to-all-start.2) | async-done | bytes 1048608 | tf_op jit(solution)/shard_map/all_to_all | solution.py:43
  498.9 1.1 broadcast_select_fusion.1
  500.0 0.0 all-reduce.9.cloned.1.call-update
  500.0 0.0 reduce-scatter.9.cloned.1.call-start
  500.1 186.0 %all-reduce.9.cloned.1.call-done = f32[512,512]{1,0:T(8,128)} async-done(((f32[512,512]{1,0:T(8,128)}), f32[512,512]{1,0:T(8,128)}) %all-reduce.9.cloned.1.call-update) | async-done | bytes 1048592 | tf_op jit(solution)/shard_map/psum | solution.py:9
  686.0 2.8 fusion.12
  688.8 0.0 reduce-scatter.9.cloned.1.call-update
  688.9 25.3 %reduce-scatter.9.cloned.1.call-done = f32[128,512]{1,0:T(8,128)} async-done(((f32[512,512]{1,0:T(8,128)}), f32[128,512]{1,0:T(8,128)}) %reduce-scatter.9.cloned.1.call-update) | async-done | bytes 262160 | tf_op jit(solution)/shard_map/reduce_scatter | solution.py:36
  714.1 2.6 fusion.2
  716.7 0.0 copy-start.5
  716.7 0.7 copy-done.5
  717.4 1.1 stack.11
  718.5 4.2 all-to-all-start.3
  722.8 0.0 all-reduce.11.cloned.1.call-start
  722.8 13.1 %all-to-all-done.3 = f32[4,128,512]{2,1,0:T(8,128)} async-done(((f32[4,128,512]{2,1,0:T(8,128)}), f32[4,128,512]{2,1,0:T(8,128)}, u32[]{:S(2)}, u32[]{:S(2)}) %all-to-all-start.3) | async-done | bytes 1048608 | tf_op jit(solution)/shard_map/all_to_all | solution.py:43
  736.0 1.1 broadcast_select_fusion
  737.1 0.0 all-reduce.11.cloned.1.call-update
  737.1 0.2 reduce-scatter.11.cloned.1.call-start
  737.3 185.1 %all-reduce.11.cloned.1.call-done = f32[512,512]{1,0:T(8,128)} async-done(((f32[512,512]{1,0:T(8,128)}), f32[512,512]{1,0:T(8,128)}) %all-reduce.11.cloned.1.call-update) | async-done | bytes 1048592 | tf_op jit(solution)/shard_map/psum | solution.py:9
  922.4 4.9 fusion
  927.3 0.0 reduce-scatter.11.cloned.1.call-update
  927.4 32.8 %reduce-scatter.11.cloned.1.call-done = f32[128,1024]{1,0:T(8,128)} async-done(((f32[512,1024]{1,0:T(8,128)}), f32[128,1024]{1,0:T(8,128)}) %reduce-scatter.11.cloned.1.call-update) | async-done | bytes 524304 | tf_op jit(solution)/shard_map/reduce_scatter | solution.py:48
  960.2 0.0 copy-done.2
  960.2 1.1 sub.15
  961.3 0.0 copy-done.4
  961.4 0.2 slice_select_fusion
  961.5 0.0 copy-start.9
  961.5 0.8 copy-done.9
  (8 shorter events, 0.0 us)
Async XLA Ops:
  9.0 1.1 copy-start.7
  10.1 18.4 %all-to-all-start = ((f32[4,128,512]{2,1,0:T(8,128)}), f32[4,128,512]{2,1,0:T(8,128)S(1)}, u32[]{:S(2)}, u32[]{:S(2)}) async-start(f32[4,128,512]{2,1,0:T(8,128)} %stack.8), calls=%async_computation | async-start | bytes 2097152 | tf_op jit(solution)/shard_map/all_to_all | solution.py:43
  15.1 201.2 %copy-start = (f32[1024,512]{1,0:T(8,128)S(1)}, f32[1024,512]{1,0:T(8,128)}, u32[]{:S(2)}) copy-start(f32[1024,512]{1,0:T(8,128)} %param.4) | copy-start | bytes 6291460
  15.1 201.2 %all-reduce.5.cloned.1.call-start = ((), (), s32[]{:S(2)}) async-start(), calls=%async_computation.8 | async-start | bytes 2097152 | tf_op jit(solution)/shard_map/psum | solution.py:9
  29.7 213.5 %reduce-scatter.5.cloned.1.call-start = ((), (), s32[]{:S(2)}) async-start(), calls=%async_computation.9 | async-start | bytes 1310720 | tf_op jit(solution)/shard_map/reduce_scatter | solution.py:36
  29.8 213.5 %copy-start.1 = (f32[128,1024]{1,0:T(8,128)S(1)}, f32[128,1024]{1,0:T(8,128)}, u32[]{:S(2)}) copy-start(f32[128,1024]{1,0:T(8,128)} %param.3) | copy-start | bytes 1572868
  246.8 16.6 %all-to-all-start.1 = ((f32[4,128,512]{2,1,0:T(8,128)}), f32[4,128,512]{2,1,0:T(8,128)S(1)}, u32[]{:S(2)}, u32[]{:S(2)}) async-start(f32[4,128,512]{2,1,0:T(8,128)} %stack.9), calls=%async_computation.2 | async-start | bytes 2097152 | tf_op jit(solution)/shard_map/all_to_all | solution.py:43
  250.3 199.7 %all-reduce.7.cloned.1.call-start = ((), (), s32[]{:S(2)}) async-start(), calls=%async_computation.10 | async-start | bytes 2097152 | tf_op jit(solution)/shard_map/psum | solution.py:9
  264.5 212.6 %reduce-scatter.7.cloned.1.call-start = ((), (), s32[]{:S(2)}) async-start(), calls=%async_computation.11 | async-start | bytes 1310720 | tf_op jit(solution)/shard_map/reduce_scatter | solution.py:36
  479.7 0.7 copy-start.3
  481.5 17.4 %all-to-all-start.2 = ((f32[4,128,512]{2,1,0:T(8,128)}), f32[4,128,512]{2,1,0:T(8,128)}, u32[]{:S(2)}, u32[]{:S(2)}) async-start(f32[4,128,512]{2,1,0:T(8,128)} %stack.10), calls=%async_computation.4 | async-start | bytes 2097152 | tf_op jit(solution)/shard_map/all_to_all | solution.py:43
  485.8 200.3 %all-reduce.9.cloned.1.call-start = ((), (), s32[]{:S(2)}) async-start(), calls=%async_computation.12 | async-start | bytes 2097152 | tf_op jit(solution)/shard_map/psum | solution.py:9
  500.0 214.1 %reduce-scatter.9.cloned.1.call-start = ((), (), s32[]{:S(2)}) async-start(), calls=%async_computation.13 | async-start | bytes 1310720 | tf_op jit(solution)/shard_map/reduce_scatter | solution.py:36
  716.7 0.7 copy-start.5
  718.5 17.4 %all-to-all-start.3 = ((f32[4,128,512]{2,1,0:T(8,128)}), f32[4,128,512]{2,1,0:T(8,128)}, u32[]{:S(2)}, u32[]{:S(2)}) async-start(f32[4,128,512]{2,1,0:T(8,128)} %stack.11), calls=%async_computation.6 | async-start | bytes 2097152 | tf_op jit(solution)/shard_map/all_to_all | solution.py:43
  722.8 199.7 %all-reduce.11.cloned.1.call-start = ((), (), s32[]{:S(2)}) async-start(), calls=%async_computation.14 | async-start | bytes 2097152 | tf_op jit(solution)/shard_map/psum | solution.py:9
  737.1 223.1 %reduce-scatter.11.cloned.1.call-start = ((), (), s32[]{:S(2)}) async-start(), calls=%async_computation.15 | async-start | bytes 2621440 | tf_op jit(solution)/shard_map/reduce_scatter | solution.py:48
  927.3 32.9 %copy-start.2 = (f32[128,1024]{1,0:T(8,128)S(1)}, f32[128,1024]{1,0:T(8,128)}, u32[]{:S(2)}) copy-start(f32[128,1024]{1,0:T(8,128)} %param.3) | copy-start | bytes 1572868
  927.3 34.0 %copy-start.4 = (f32[128,512]{1,0:T(8,128)S(1)}, f32[128,512]{1,0:T(8,128)}, u32[]{:S(2)}) copy-start(f32[128,512]{1,0:T(8,128)} %copy-done.3) | copy-start | bytes 786436
  927.3 34.0 %copy-start.6 = (f32[128,512]{1,0:T(8,128)S(1)}, f32[128,512]{1,0:T(8,128)}, u32[]{:S(2)}) copy-start(f32[128,512]{1,0:T(8,128)} %copy-done.5) | copy-start | bytes 786436
  927.3 34.0 %copy-start.8 = (f32[128,512]{1,0:T(8,128)S(1)}, f32[128,512]{1,0:T(8,128)}, u32[]{:S(2)}) copy-start(f32[128,512]{1,0:T(8,128)} %copy-done.7) | copy-start | bytes 786436
  961.5 0.8 copy-start.9
Sparse Core Ops, SparseCore 0:
  29.8 186.4 all-reduce.4
  220.5 22.6 reduce-scatter.4
  264.6 185.3 all-reduce.6
  454.5 22.6 reduce-scatter.6
  500.1 185.8 all-reduce.8
  689.0 25.1 reduce-scatter.8
  737.2 185.1 all-reduce.10
  927.5 32.6 reduce-scatter.10
